TPU v7x, 128 devices: a whole 4x4x4 slice. The times are simulated.
128 devices in a mesh: blk: 32 (over y, x, core), grp: 4 (over z).
Axes of the slice: x: 4, y: 4, z: 4, core: 2. Of those that a mesh axis runs over, the one named last changes fastest.
Arguments:
- sky_map: bfloat16 [256, 1048576], P(None, ('blk', 'grp')), may hold values from -128 to 128
- fg_templates: bfloat16 [256, 16], replicated, may hold values from -0.375 to 0.375
- cycle_len: int32 [512], P(('blk', 'grp')), may hold values from 512 to 2048, as said below
- beam_profile: float32 [8, 1024], replicated, may hold values from 0.2 to 2
- beam_index: int32 [256], P('blk'), may hold values from 0 to 7
Outputs:
- filtered: float32 [1024, 256, 2, 1024], P(None, 'blk', None, 'grp')
Inputs may be any that keep to these rules, and one draw needn't show every extreme that they name: `cycle_len`: some cycle has exactly 2048 pixels.
All inputs are finite; a program needn't handle non-finite values.
Results may differ from a plain program's by a relative error of at most 0.0064.
Values may be sent and summed in bfloat16 or wider, within the bound.
No kernel may reach another device: no remote copies, remote signals or barrier semaphores. Data moves between devices by JAX's collectives and lax.ppermute only.
A program may use at most 192 MiB of HBM per device.

v0:
```python
import jax
import jax.numpy as jnp
from jax import lax
from jax.sharding import PartitionSpec as P

RPIX = 2048
L = 1024
M_DEV = 256


def cycle_table(length, m_width):
    slots = jnp.arange(RPIX, dtype=jnp.int32)
    orders = jnp.arange(m_width, dtype=jnp.int32)
    phase = orders[None, :] * (2 * slots[:, None] + 1) % (2 * length)
    angle = jnp.pi * phase.astype(jnp.float32) / length.astype(jnp.float32)
    weight = jnp.where(slots < length, 1.0, 0.0).astype(jnp.float32) * lax.rsqrt(
        length.astype(jnp.float32)
    )
    table = jnp.concatenate([jnp.cos(angle), -jnp.sin(angle)], axis=1) * weight[:, None]
    return table.astype(jnp.bfloat16)


def theta_table(cycle_ids, n_cycle):
    degrees = jnp.arange(L, dtype=jnp.int32)
    odd = 2 * cycle_ids + 1
    phase = degrees[:, None] * odd[None, :] % (4 * n_cycle)
    angle = jnp.pi * phase.astype(jnp.float32) / (2.0 * n_cycle)
    weight = jnp.sin(jnp.pi * odd.astype(jnp.float32) / (2.0 * n_cycle)) * (
        2.0 / jnp.sqrt(jnp.float32(n_cycle))
    )
    return (jnp.cos(angle) * weight[None, :]).astype(jnp.bfloat16)


def body(sky_map, fg_templates, cycle_len, beam_profile, beam_index):
    n_blk = lax.axis_size("blk")
    n_grp = lax.axis_size("grp")
    cycle_dev = cycle_len.shape[0]
    n_chan = sky_map.shape[0]
    chan_dev = n_chan // n_blk
    m_width = M_DEV * n_grp
    n_cycle = cycle_dev * n_blk * n_grp
    slots = jnp.arange(RPIX, dtype=jnp.int32)
    valid = (slots[None, :] < cycle_len[:, None]).reshape(-1)
    masked = jnp.where(valid[None, :], sky_map, jnp.zeros((), jnp.bfloat16))
    mode_amps = jnp.dot(fg_templates.T, masked, preferred_element_type=jnp.float32).astype(
        jnp.bfloat16
    )
    gram_part = jnp.dot(mode_amps, mode_amps.T, preferred_element_type=jnp.float32)
    cross_part = lax.dot_general(
        mode_amps, masked, (((1,), (1,)), ((), ())), preferred_element_type=jnp.float32
    )
    amps_wide = mode_amps.astype(jnp.float32)
    gram_sum = lax.psum(gram_part, ("blk", "grp"))
    lower = jnp.linalg.cholesky(gram_sum)
    basis = jax.scipy.linalg.solve_triangular(lower, amps_wide, lower=True)
    proj_part = jax.scipy.linalg.solve_triangular(lower, cross_part, lower=True)
    projected = lax.psum(proj_part, ("blk", "grp"))
    correction = jnp.dot(projected.T, basis, precision=lax.Precision.HIGHEST)
    cleaned = (masked.astype(jnp.float32) - correction).astype(jnp.bfloat16)
    pieces = []
    for local in range(cycle_dev):
        block = cleaned[:, local * RPIX : (local + 1) * RPIX]
        table = cycle_table(cycle_len[local], m_width)
        pieces.append(
            jnp.dot(block, table, preferred_element_type=jnp.float32).astype(jnp.bfloat16)
        )
    fourier = jnp.stack(pieces, 0).reshape(cycle_dev, n_chan, 2, m_width)
    position = jnp.arange(n_cycle, dtype=jnp.int32)
    moved = lax.all_to_all(
        lax.all_to_all(fourier, "blk", split_axis=1, concat_axis=0, tiled=True),
        "grp",
        split_axis=3,
        concat_axis=0,
        tiled=True,
    )
    group_id = position // (n_blk * cycle_dev)
    block_id = position // cycle_dev % n_blk
    cycle_ids = (block_id * n_grp + group_id) * cycle_dev + position % cycle_dev
    moved = moved.reshape(n_cycle, chan_dev * 2 * M_DEV)
    theta_tab = theta_table(cycle_ids, n_cycle)
    harmonic = jnp.dot(theta_tab, moved, preferred_element_type=jnp.float32).reshape(
        L, chan_dev, 2, M_DEV
    )
    onehot = (
        beam_index[:, None] == jnp.arange(beam_profile.shape[0], dtype=jnp.int32)[None, :]
    ).astype(jnp.float32)
    profiles = jnp.dot(onehot, beam_profile, precision=lax.Precision.HIGHEST)
    shaped = harmonic * profiles.T[:, :, None, None]
    orders = lax.axis_index("grp") * M_DEV + jnp.arange(M_DEV, dtype=jnp.int32)
    mweight = 0.25 + orders.astype(jnp.float32) / m_width
    weighted = shaped * mweight[None, None, None, :]
    power_part = jnp.sum(weighted * weighted, axis=(0, 2, 3))
    power = lax.psum(power_part, "grp")
    return weighted * lax.rsqrt(power / (2.0 * L * m_width) + 1e-06)[None, :, None, None]


def solution(mesh):
    return jax.shard_map(
        body,
        mesh=mesh,
        in_specs=(P(None, ("blk", "grp")), P(), P(("blk", "grp")), P(), P("blk")),
        out_specs=P(None, "blk", None, "grp"),
        check_vma=False,
    )
```

profile of v0, /device:TPU:0, one launch (start us, length us, event | category | flops | bytes accessed | tf_op | source)
XLA Modules:
  0.0 859.5 jit_solution(13465190245039165098)
XLA Ops:
  0.0 0.0 copy-start
  0.0 1.4 fusion.120
  6.2 0.7 fusion.87
  7.0 2.9 convolution_convert_fusion
  9.9 0.2 fusion.121
  10.1 3.4 fusion.50
  13.5 68.2 %psum.21 = f32[16,16]{0,1:T(8,128)S(1)} all-reduce(f32[16,16]{0,1:T(8,128)S(1)} %fusion.121), channel_id=1, replica_groups=mesh['blk'=32,'grp'=4] {'blk','grp'}, use_global_device_ids=true, to_apply=%region_0.1 | all-reduce | flops 256 | bytes 2048 | tf_op jit(solution)/shard_map/psum | solution.py:53
  81.7 0.1 copy.38
  81.8 1.5 cholesky.16
  83.3 0.7 compare_reduce_fusion
  84.0 0.7 fusion.88
  84.7 1.2 custom-call.10
  85.9 0.4 fusion.89
  86.3 0.2 fusion.91
  86.5 62.3 %psum.22 = f32[16,256]{1,0:T(8,128)S(1)} all-reduce(f32[16,256]{1,0:T(8,128)S(1)} %fusion.91), channel_id=1, replica_groups=mesh['blk'=32,'grp'=4] {'blk','grp'}, use_global_device_ids=true, to_apply=%region_3.4 | all-reduce | flops 4096 | bytes 32768 | tf_op jit(solution)/shard_map/psum | solution.py:57
  148.9 0.7 select_multiply_fusion.3
  149.6 8.9 %fusion.5 = bf16[256,8192]{1,0:T(8,128)(2,1)S(1)} fusion(f32[16,256]{1,0:T(8,128)S(1)} %psum.22, f32[16,8192]{1,0:T(8,128)S(1)} %fusion.89, bf16[256,8192]{1,0:T(8,128)(2,1)} %param.5, pred[8192]{0:T(1024)(128)(4,1)S(1)} %bitcast.62), kind=kOutput, calls=%fused_computation.16 | convolution fusion | flops 411041792 | bytes 8937472 | tf_op jit(solution)/shard_map/dot_general | solution.py:58
  158.5 0.0 copy-start.1
  158.5 451.2 %fusion.49 = (f32[2048,1024]{1,0:T(8,128)S(1)}, f32[2048,1024]{1,0:T(8,128)}, f32[2048,1024]{1,0:T(8,128)}, f32[2048,1024]{1,0:T(8,128)}, f32[2048,1024]{1,0:T(8...) fusion(f32[]{:T(128)S(6)} %convert_element_type.91, pred[]{:T(512)S(6)} %lt.110, ...), kind=kLoop, calls=%fused_computation.64 | loop fusion | flops 94371840 | bytes 67117088 | tf_op jit(solution)/shard_map/cos | solution.py:19
  609.7 0.0 copy-done.1
  609.7 6.3 fusion.51
  616.0 0.8 stack.15
  616.8 0.6 select_multiply_fusion.2
  617.4 8.5 fusion.54
  626.0 0.8 stack.16
  626.8 0.6 select_multiply_fusion.1
  627.4 9.5 %fusion.57 = bf16[256,2048]{1,0:T(8,128)(2,1)} fusion(f32[2048,1024]{1,0:T(8,128)} %get-tuple-element.7, f32[2048,1024]{1,0:T(8,128)} %get-tuple-element.10, f32[2048]{0:T(1024)S(1)} %select_multiply_fusion.1, bf16[256,8192]{1,0:T(8,128)(2,1)} %copy-done.1), kind=kOutput, calls=%fused_computation.72 | convolution fusion | flops 2160590848 | bytes 18882560 | tf_op jit(solution)/shard_map/dot_general | solution.py:65
  636.9 1.8 stack.17
  638.7 0.6 select_multiply_fusion
  639.3 9.5 %fusion.60 = bf16[256,2048]{1,0:T(8,128)(2,1)} fusion(f32[2048,1024]{1,0:T(8,128)} %get-tuple-element.8, f32[2048,1024]{1,0:T(8,128)} %get-tuple-element.9, f32[2048]{0:T(1024)S(1)} %select_multiply_fusion, bf16[256,8192]{1,0:T(8,128)(2,1)} %copy-done.1), kind=kOutput, calls=%fused_computation.73 | convolution fusion | flops 2160590848 | bytes 18882560 | tf_op jit(solution)/shard_map/dot_general | solution.py:65
  648.8 2.6 stack.18
  651.4 7.6 pad_maximum_fusion
  659.0 55.9 %all_to_all.33 = bf16[4,256,2,1024]{3,2,0,1:T(2,128)(2,1)S(1)} all-to-all(bf16[4,256,2,1024]{3,2,0,1:T(2,128)(2,1)S(1)} %pad_maximum_fusion), channel_id=1, replica_groups=mesh['blk'=32,'grp'=4] {'blk'}, dimensions={1} | all-to-all | bytes 8388608 | tf_op jit(solution)/shard_map/all_to_all | solution.py:70
  714.9 2.3 copy.55
  717.3 2.5 copy.44
  719.7 0.0 copy-start.2
  719.7 7.3 copy.45
  727.0 4.9 all-to-all-start.1
  731.9 0.1 sine_multiply_fusion
  732.0 0.0 copy-done
  732.0 0.0 copy-done.2
  732.0 0.2 convolution_bitcast_fusion
  732.2 49.1 %all-to-all-done.1 = bf16[128,8,2,1024]{0,1,2,3:T(8,128)(2,1)} async-done(((bf16[128,8,2,1024]{0,1,2,3:T(8,128)(2,1)}), bf16[128,8,2,1024]{0,1,2,3:T(8,128)(2,1)}, u32[]{:S(2)}, u32[]{:S(2)}) %all-to-all-start.1) | async-done | bytes 4194336 | tf_op jit(solution)/shard_map/all_to_all | solution.py:69
  781.3 9.0 %copy.47 = bf16[4,128,8,2,256]{4,3,2,1,0:T(2,128)(2,1)} copy(bf16[4,128,8,2,256]{1,2,3,4,0:T(8,128)(2,1)} %bitcast.18) | data formatting | bytes 8388608 | tf_op jit(solution)/shard_map/all_to_all | solution.py:69
  790.3 7.8 reshape.135
  798.1 6.5 copy.48
  804.6 17.2 %multiply_reduce_fusion = (f32[8]{0:T(128)S(1)}, f32[1024,8,2,256]{3,0,2,1:T(8,128)}) fusion(f32[256]{0:T(256)S(1)} %multiply_add_fusion.1, f32[1024,8]{0,1:T(8,128)S(1)} %convolution_bitcast_fusion, bf16[8,2,256,512]{3,2,1,0:T(8,128)(2,1)} %bitcast.55, f32[512]{0:T(512)S(1)} %sine_multiply_fusion, s32[512]{0:T(512)S(1)} %fusion.104), kind=kOutput, calls=%fused_computation.8 | convolution fusion | flops 4320133120 | bytes 21009440 | tf_op jit(solution)/shard_map/dot_general | solution.py:81
  821.9 8.8 %psum.23 = f32[8]{0:T(128)S(1)} all-reduce(f32[8]{0:T(128)S(1)} %get-tuple-element.17), channel_id=1, replica_groups=mesh['blk'=32,'grp'=4] {'grp'}, use_global_device_ids=true, to_apply=%region_5.6 | all-reduce | flops 8 | bytes 64 | tf_op jit(solution)/shard_map/psum | solution.py:93
  830.7 7.0 fusion.4
  837.8 21.5 %copy.49 = f32[1024,8,2,256]{3,2,1,0:T(2,128)} copy(f32[1024,8,2,256]{3,0,2,1:T(8,128)S(1)} %fusion.4) | data formatting | bytes 33554432 | tf_op jit(solution)/shard_map/mul | solution.py:94
  (7 shorter events, 0.1 us)
Async XLA Ops:
  0.0 732.0 %copy-start = (f32[8,1024]{1,0:T(8,128)S(1)}, f32[8,1024]{1,0:T(8,128)}, u32[]{:S(2)}) copy-start(f32[8,1024]{1,0:T(8,128)} %param.8) | copy-start | bytes 98308
  158.5 451.2 %copy-start.1 = (bf16[256,8192]{1,0:T(8,128)(2,1)}, bf16[256,8192]{1,0:T(8,128)(2,1)S(1)}, u32[]{:S(2)}) copy-start(bf16[256,8192]{1,0:T(8,128)(2,1)S(1)} %fusion.5) | copy-start | bytes 12582916
  719.7 12.3 %copy-start.2 = (s32[8]{0:T(128)S(1)}, s32[8]{0:T(128)}, u32[]{:S(2)}) copy-start(s32[8]{0:T(128)} %param.9) | copy-start | bytes 100
  727.0 54.3 %all-to-all-start.1 = ((bf16[128,8,2,1024]{0,1,2,3:T(8,128)(2,1)}), bf16[128,8,2,1024]{0,1,2,3:T(8,128)(2,1)}, u32[]{:S(2)}, u32[]{:S(2)}) async-start(bf16[128,8,2,1024]{0,1,2,3:T(8,128)(2,1)} %copy.45), calls=%async_computation.1 | async-start | bytes 8388608 | tf_op jit(solution)/shard_map/all_to_all | solution.py:69
where the time goes:
time: 867 us; the launch traced here: 859 us
  other arithmetic  473 us (55%)
  blocking collectives  195 us (22%)
  matrix products  67.2 us (8%)
  local copies, waits for them, and re-layouts  64.4 us (7%)
  waiting for transfers between devices  49.1 us (6%)
    cos x1, other arithmetic, cycle_table(): jnp.cos(angle)  451 us
    psum x1, blocking collectives, body(): gram_sum = lax.psum(gram_part, ('blk', 'grp'))  68.2 us
    psum x1, blocking collectives, body(): projected = lax.psum(proj_part, ('blk', 'grp'))  62.3 us
    all_to_all x1, blocking collectives, body(): lax.all_to_all(fourier, 'blk', split_axis=1, concat_axis=0, tiled=True)  55.9 us
    all_to_all x1, waiting for transfers between devices, body(): lax.all_to_all(lax.all_to_all(fourier, 'blk', split_axis=1, concat_axis=0...  49.1 us
    dot_general x4, matrix products, body(): jnp.dot(block, table, preferred_element_type=jnp.float32)  33.9 us
    mul x1, local copies, waits for them, and re-layouts, body(): weighted * lax.rsqrt(power / (2.0 * L * m_width) + 1e-06)[None, :, None,...  21.5 us
  transfers between devices with their start and end apart: 1, of which 1 were waited for; matrix products, arithmetic and copies ran while one was open for 0% of the time, Pallas kernels for 0%

commit v1 on v0

--- a/solution.py
+++ b/solution.py
@@ -54,7 +54,7 @@
     lower = jnp.linalg.cholesky(gram_sum)
     basis = jax.scipy.linalg.solve_triangular(lower, amps_wide, lower=True)
     proj_part = jax.scipy.linalg.solve_triangular(lower, cross_part, lower=True)
-    projected = lax.psum(proj_part, ("blk", "grp"))
+    projected = jnp.sum(lax.all_gather(proj_part, ("blk", "grp")), axis=0)
     correction = jnp.dot(projected.T, basis, precision=lax.Precision.HIGHEST)
     cleaned = (masked.astype(jnp.float32) - correction).astype(jnp.bfloat16)
     pieces = []

time: 867 us -> 819 us (0.945)
  blocking collectives: 195 us -> 132 us
  between operations: 5.45 us -> 18.9 us
    psum x1 -> x0, blocking collectives: 62.3 us -> none  [body(): projected = lax.psum(proj_part, ('blk', 'grp'))]
  transfers between devices with their start and end apart: 1 -> 2, of which waited for: 1 -> 1; matrix products, arithmetic and copies ran while one was open for 0% -> 56% of each run, Pallas kernels for 0% -> 0%
where the time goes in v1:
time: 819 us; the launch traced here: 817 us
  other arithmetic  479 us (58%)
  blocking collectives  132 us (16%)
  matrix products  68.2 us (8%)
  local copies, waits for them, and re-layouts  65.6 us (8%)
  waiting for transfers between devices  49.2 us (6%)
  between operations  18.9 us (2%)
    cos x1, other arithmetic, cycle_table(): jnp.cos(angle)  455 us
    psum x1, blocking collectives, body(): gram_sum = lax.psum(gram_part, ('blk', 'grp'))  68.2 us
    all_to_all x1, blocking collectives, body(): lax.all_to_all(fourier, 'blk', split_axis=1, concat_axis=0, tiled=True)  55 us
    all_to_all x1, waiting for transfers between devices, body(): lax.all_to_all(lax.all_to_all(fourier, 'blk', split_axis=1, concat_axis=0...  49.1 us
    dot_general x4, matrix products, body(): jnp.dot(block, table, preferred_element_type=jnp.float32)  33.8 us
    mul x1, local copies, waits for them, and re-layouts, body(): weighted * lax.rsqrt(power / (2.0 * L * m_width) + 1e-06)[None, :, None,...  21.5 us
    dot_general x1, matrix products, body(): jnp.dot(theta_tab, moved, preferred_element_type=jnp.float32)  17.2 us
  transfers between devices with their start and end apart: 2, of which 1 were waited for; matrix products, arithmetic and copies ran while one was open for 56% of the time, Pallas kernels for 0%

profile of v1, /device:TPU:0, one launch (start us, length us, event | category | flops | bytes accessed | tf_op | source)
XLA Modules:
  0.0 817.3 jit_solution(11022977768885917442)
XLA Ops:
  6.5 0.0 copy-start
  6.5 0.0 copy-start.3
  6.5 0.0 all-gather.3.cloned.1.call-start
  6.5 0.8 fusion.87
  7.4 2.9 convolution_convert_fusion
  10.2 0.2 fusion.121
  10.5 3.4 fusion.50
  13.8 68.2 %psum.14 = f32[16,16]{0,1:T(8,128)S(1)} all-reduce(f32[16,16]{0,1:T(8,128)S(1)} %fusion.121), channel_id=1, replica_groups=mesh['blk'=32,'grp'=4] {'blk','grp'}, use_global_device_ids=true, to_apply=%region_0.1 | all-reduce | flops 256 | bytes 2048 | tf_op jit(solution)/shard_map/psum | solution.py:53
  82.1 0.1 copy.38
  82.1 1.5 cholesky.16
  83.6 0.6 compare_reduce_fusion
  84.3 0.6 fusion.88
  84.9 1.2 custom-call.10
  86.2 0.8 fusion.91
  87.0 0.0 all-gather.3.cloned.1.call-update
  87.0 0.0 copy-done.3
  87.0 0.7 fusion.120
  92.8 0.4 fusion.89
  93.3 0.7 select_multiply_fusion.3
  94.0 0.7 select_multiply_fusion.2
  94.7 0.6 select_multiply_fusion.1
  95.4 0.6 select_multiply_fusion
  96.0 454.7 %fusion.49 = (f32[2048,1024]{1,0:T(8,128)}, f32[2048,1024]{1,0:T(8,128)}, f32[2048,1024]{1,0:T(8,128)}, f32[2048,1024]{1,0:T(8,128)}, f32[2048,1024]{1,0:T(8,128...) fusion(f32[]{:T(128)S(6)} %convert_element_type.91, pred[]{:T(512)S(6)} %lt.110, ...), kind=kLoop, calls=%fused_computation.64 | loop fusion | flops 94371840 | bytes 67117088 | tf_op jit(solution)/shard_map/cos | solution.py:19
  550.7 0.0 all-gather.3.cloned.1.call-done
  550.7 1.8 reduce_sum.18
  552.5 0.0 copy-start.1
  552.5 9.2 %fusion.5 = bf16[256,8192]{1,0:T(8,128)(2,1)S(1)} fusion(f32[16,256]{1,0:T(8,128)S(1)} %reduce_sum.18, f32[16,8192]{1,0:T(8,128)S(1)} %fusion.89, bf16[256,8192]{1,0:T(8,128)(2,1)} %param.5, pred[8192]{0:T(1024)(128)(4,1)S(1)} %bitcast.64), kind=kOutput, calls=%fused_computation.16 | convolution fusion | flops 411041792 | bytes 8937472 | tf_op jit(solution)/shard_map/dot_general | solution.py:58
  561.7 0.0 copy-start.2
  561.7 1.9 copy-done.2
  563.6 0.0 copy-done.1
  563.6 6.3 fusion.51
  569.9 0.8 stack.15
  570.7 8.5 %fusion.54 = bf16[256,2048]{1,0:T(8,128)(2,1)S(1)} fusion(f32[2048,1024]{1,0:T(8,128)} %get-tuple-element.6, f32[2048,1024]{1,0:T(8,128)} %get-tuple-element.11, f32[2048]{0:T(1024)S(1)} %select_multiply_fusion.2, bf16[256,8192]{1,0:T(8,128)(2,1)} %copy-done.2), kind=kOutput, calls=%fused_computation.71 | convolution fusion | flops 2160590848 | bytes 18882560 | tf_op jit(solution)/shard_map/dot_general | solution.py:65
  579.2 0.8 stack.16
  580.0 9.5 %fusion.57 = bf16[256,2048]{1,0:T(8,128)(2,1)} fusion(f32[2048,1024]{1,0:T(8,128)} %get-tuple-element.7, f32[2048,1024]{1,0:T(8,128)} %get-tuple-element.10, f32[2048]{0:T(1024)S(1)} %select_multiply_fusion.1, bf16[256,8192]{1,0:T(8,128)(2,1)} %copy-done.2), kind=kOutput, calls=%fused_computation.72 | convolution fusion | flops 2160590848 | bytes 18882560 | tf_op jit(solution)/shard_map/dot_general | solution.py:65
  589.6 1.8 stack.17
  591.4 9.5 %fusion.60 = bf16[256,2048]{1,0:T(8,128)(2,1)} fusion(f32[2048,1024]{1,0:T(8,128)} %get-tuple-element.8, f32[2048,1024]{1,0:T(8,128)} %get-tuple-element.9, f32[2048]{0:T(1024)S(1)} %select_multiply_fusion, bf16[256,8192]{1,0:T(8,128)(2,1)} %copy-done.2), kind=kOutput, calls=%fused_computation.73 | convolution fusion | flops 2160590848 | bytes 18882560 | tf_op jit(solution)/shard_map/dot_general | solution.py:65
  600.9 2.6 stack.18
  603.5 7.6 pad_maximum_fusion
  611.1 55.0 %all_to_all.33 = bf16[4,256,2,1024]{3,2,0,1:T(2,128)(2,1)S(1)} all-to-all(bf16[4,256,2,1024]{3,2,0,1:T(2,128)(2,1)S(1)} %pad_maximum_fusion), channel_id=1, replica_groups=mesh['blk'=32,'grp'=4] {'blk'}, dimensions={1} | all-to-all | bytes 8388608 | tf_op jit(solution)/shard_map/all_to_all | solution.py:70
  666.1 2.3 copy.55
  668.4 2.5 copy.44
  670.9 0.0 copy-start.4
  670.9 7.3 copy.45
  678.2 4.9 all-to-all-start.1
  683.1 0.1 sine_multiply_fusion
  683.2 0.0 copy-done
  683.2 0.0 copy-done.4
  683.2 0.2 convolution_bitcast_fusion
  683.4 49.1 %all-to-all-done.1 = bf16[128,8,2,1024]{0,1,2,3:T(8,128)(2,1)} async-done(((bf16[128,8,2,1024]{0,1,2,3:T(8,128)(2,1)}), bf16[128,8,2,1024]{0,1,2,3:T(8,128)(2,1)}, u32[]{:S(2)}, u32[]{:S(2)}) %all-to-all-start.1) | async-done | bytes 4194336 | tf_op jit(solution)/shard_map/all_to_all | solution.py:69
  732.5 9.0 %copy.47 = bf16[4,128,8,2,256]{4,3,2,1,0:T(2,128)(2,1)} copy(bf16[4,128,8,2,256]{1,2,3,4,0:T(8,128)(2,1)} %bitcast.19) | data formatting | bytes 8388608 | tf_op jit(solution)/shard_map/all_to_all | solution.py:69
  741.5 7.8 reshape.135
  749.3 6.5 copy.48
  755.8 17.2 %multiply_reduce_fusion = (f32[8]{0:T(128)S(1)}, f32[1024,8,2,256]{3,0,2,1:T(8,128)}) fusion(f32[256]{0:T(256)S(1)} %multiply_add_fusion.1, f32[1024,8]{0,1:T(8,128)S(1)} %convolution_bitcast_fusion, bf16[8,2,256,512]{3,2,1,0:T(8,128)(2,1)} %bitcast.56, f32[512]{0:T(512)S(1)} %sine_multiply_fusion, s32[512]{0:T(512)S(1)} %fusion.104), kind=kOutput, calls=%fused_computation.8 | convolution fusion | flops 4320133120 | bytes 21009440 | tf_op jit(solution)/shard_map/dot_general | solution.py:81
  773.0 8.9 %psum.15 = f32[8]{0:T(128)S(1)} all-reduce(f32[8]{0:T(128)S(1)} %get-tuple-element.17), channel_id=1, replica_groups=mesh['blk'=32,'grp'=4] {'grp'}, use_global_device_ids=true, to_apply=%region_5.6 | all-reduce | flops 8 | bytes 64 | tf_op jit(solution)/shard_map/psum | solution.py:93
  781.9 7.0 fusion.4
  788.9 21.5 %copy.49 = f32[1024,8,2,256]{3,2,1,0:T(2,128)} copy(f32[1024,8,2,256]{3,0,2,1:T(8,128)S(1)} %fusion.4) | data formatting | bytes 33554432 | tf_op jit(solution)/shard_map/mul | solution.py:94
  (7 shorter events, 0.1 us)
Async XLA Ops:
  6.5 676.6 %copy-start = (f32[8,1024]{1,0:T(8,128)S(1)}, f32[8,1024]{1,0:T(8,128)}, u32[]{:S(2)}) copy-start(f32[8,1024]{1,0:T(8,128)} %param.8) | copy-start | bytes 98308
  6.5 80.5 %copy-start.3 = (s32[4]{0:T(128)S(1)}, s32[4]{0:T(128)}, u32[]{:S(2)}) copy-start(s32[4]{0:T(128)} %param.7) | copy-start | bytes 52
  6.5 544.2 %all-gather.3.cloned.1.call-start = ((), (), s32[]{:S(2)}) async-start(), calls=%async_computation.2 | async-start | bytes 2113536 | tf_op jit(solution)/shard_map/all_gather | solution.py:57
  552.5 11.1 %copy-start.1 = (f32[2048,1024]{1,0:T(8,128)S(1)}, f32[2048,1024]{1,0:T(8,128)}, u32[]{:S(2)}) copy-start(f32[2048,1024]{1,0:T(8,128)} %get-tuple-element.5) | copy-start | bytes 25165828
  561.7 1.9 copy-start.2
  670.9 12.3 %copy-start.4 = (s32[8]{0:T(128)S(1)}, s32[8]{0:T(128)}, u32[]{:S(2)}) copy-start(s32[8]{0:T(128)} %param.9) | copy-start | bytes 100
  678.2 54.3 %all-to-all-start.1 = ((bf16[128,8,2,1024]{0,1,2,3:T(8,128)(2,1)}), bf16[128,8,2,1024]{0,1,2,3:T(8,128)(2,1)}, u32[]{:S(2)}, u32[]{:S(2)}) async-start(bf16[128,8,2,1024]{0,1,2,3:T(8,128)(2,1)} %copy.45), calls=%async_computation.1 | async-start | bytes 8388608 | tf_op jit(solution)/shard_map/all_to_all | solution.py:69
Sparse Core Ops, SparseCore 0:
  87.1 61.5 all-gather.2
